TPU v7x, 512 devices: a whole 4x8x8 slice. The times are simulated.
512 devices in a mesh: grp: 16 (over z, core), shard: 32 (over x, y).
Axes of the slice: x: 4, y: 8, z: 8, core: 2. Of those that a mesh axis runs over, the one named last changes fastest.
Arguments:
- src_rows: bfloat16 [128, 128, 5376], P('grp', 'shard'), may hold values from -6 to 6
- src_act: bfloat16 [128, 128], P('grp', 'shard'), may hold values from 0.29882812 to 3
- encoder: bfloat16 [16, 32, 3, 5376, 128], P('grp', 'shard'), may hold values from -0.078125 to 0.078125
- dest_list: int32 [16, 6], replicated, may hold values from -1 to 127, as said below
- pair_list: int32 [16, 32, 18, 2], P('grp', 'shard'), may hold values from 0 to 5, as said below
- pair_count: int32 [16, 32], P('grp', 'shard'), may hold values from 1 to 18, as said below
Outputs:
- edges: bfloat16 [16, 32, 18, 128, 128], P('grp', 'shard')
Inputs may be any that keep to these rules, and one draw needn't show every extreme that they name: `dest_list`: row g holds between 3 and 6 source blocks followed by -1; the blocks of one row come from distinct source groups (block // 8); some row is full. `pair_list`: entries are (slot, encoder block) with slot < 6 and block < 3; the first pair_count entries of a device are distinct pairs whose slot holds a block of its group. `pair_count`: at most 3 times the number of blocks of the device's group; some device has 18.
All inputs are finite; a program needn't handle non-finite values.
Results may differ from a plain program's by a relative error of at most 0.001.
Values may be sent and summed in bfloat16 or wider, within the bound.
No kernel may reach another device: no remote copies, remote signals or barrier semaphores. Data moves between devices by JAX's collectives and lax.ppermute only.
A program may use at most 64 MiB of HBM per device.

v0:
```python
import jax
import jax.numpy as jnp
from jax import lax
from jax.sharding import PartitionSpec as P


def local(src_rows, src_act, encoder, dest_list, pair_list, pair_count):
    my_group = lax.axis_index("grp")
    my_list = lax.dynamic_index_in_dim(dest_list, my_group, 0, keepdims=False)
    is_valid = my_list >= 0
    picked = jnp.maximum(my_list, 0)
    all_rows, all_scale = (
        lax.all_gather(src_rows, "grp", axis=0, tiled=True),
        lax.all_gather(src_act, "grp", axis=0, tiled=True),
    )
    slot_rows = jnp.take(all_rows, picked, axis=0)
    slot_scale = jnp.take(all_scale, picked, axis=0)
    slot_rows = jnp.where(is_valid[:, None, None], slot_rows, jnp.zeros((), slot_rows.dtype))
    slot_scale = jnp.where(is_valid[:, None], slot_scale, jnp.zeros((), slot_scale.dtype))
    full_rows, full_scale = (
        lax.all_gather(slot_rows, "shard", axis=1, tiled=True),
        lax.all_gather(slot_scale, "shard", axis=1, tiled=True),
    )
    weights = encoder[0, 0]
    dev_pairs = pair_list[0, 0]
    slot_ids = dev_pairs[:, 0]
    block_ids = dev_pairs[:, 1]
    amount = pair_count[0, 0]
    slots_total = full_rows.shape[0]
    tile_rows = full_rows.shape[1]
    width = full_rows.shape[2]
    enc_count = weights.shape[0]
    tile_cols = weights.shape[2]
    pair_total = dev_pairs.shape[0]
    stacked = full_rows.reshape(slots_total * tile_rows, width)
    products = jnp.einsum("rd,edc->rec", stacked, weights, preferred_element_type=jnp.float32)
    products = products.reshape(slots_total, tile_rows, enc_count, tile_cols)
    chosen = products[slot_ids, :, block_ids, :]
    scales = jnp.take(full_scale, slot_ids, axis=0).astype(jnp.float32)
    is_live = jnp.arange(pair_total) < amount
    result = jnp.where(
        is_live[:, None, None], scales[:, :, None] * chosen, jnp.zeros((), jnp.float32)
    ).astype(jnp.bfloat16)
    return result[None, None]


def solution(mesh):
    return jax.shard_map(
        local,
        mesh=mesh,
        in_specs=(
            P("grp", "shard", None),
            P("grp", "shard"),
            P("grp", "shard", None, None, None),
            P(),
            P("grp", "shard", None, None),
            P("grp", "shard"),
        ),
        out_specs=P("grp", "shard", None, None, None),
        check_vma=False,
    )
```

profile of v0, /device:TPU:1, one launch (start us, length us, event | category | flops | bytes accessed | tf_op | source)
XLA Modules:
  0.0 197.3 jit_solution(8817233090064426488)
XLA Ops:
  6.5 0.0 copy-start
  6.5 0.0 all-gather.5.cloned.1.call-start
  6.5 0.7 all-gather.5.cloned.1.call-update
  7.3 0.0 copy-start.1
  7.3 0.0 all-gather.7.cloned.1.call-start
  7.3 0.9 maximum_reduce_fusion
  8.2 0.9 compare_reduce_fusion.1
  9.1 53.5 %all-gather.5.cloned.1.call-done = bf16[128,4,5376]{2,1,0:T(4,128)(2,1)} async-done(((bf16[8,4,5376]{2,1,0:T(4,128)(2,1)}), bf16[128,4,5376]{2,1,0:T(4,128)(2,1)}) %all-gather.5.cloned.1.call-update) | async-done | bytes 5505040 | tf_op jit(solution)/shard_map/all_gather | solution.py:13
  62.6 3.3 %gather_fusion.2 = bf16[6,4,5376]{2,1,0:T(4,128)(2,1)S(1)} fusion(bf16[128,4,5376]{2,1,0:T(4,128)(2,1)} %all-gather.5.cloned.1.call-done, s32[1024]{0:T(1024)S(1)} %pad_clamp_fusion.1), kind=kCustom, calls=%fused_computation.2 | custom fusion | bytes 516120 | tf_op jit(solution)/shard_map/jit(_take)/gather | solution.py:16
  65.9 0.2 select_select_fusion
  66.2 0.8 copy.16
  66.9 0.0 all-gather.7.cloned.1.call-update
  67.0 0.0 copy-done
  67.0 16.3 %all-gather = bf16[16,8,4]{1,2,0:T(4,128)(2,1)S(1)} all-gather(bf16[1,8,4]{1,2,0:T(4,128)(2,1)S(1)} %bitcast.32), channel_id=1, replica_groups=mesh['grp'=16,'shard'=32] {'grp'}, dimensions={0}, use_global_device_ids=true | all-gather | bytes 1088 | tf_op jit(solution)/shard_map/all_gather | solution.py:14
  83.3 0.2 copy.13
  83.5 0.6 gather_fusion
  84.0 0.1 select_bitcast_fusion
  84.1 0.1 copy.14
  84.2 33.3 %all-gather.1 = bf16[32,4,6]{2,1,0:T(4,128)(2,1)S(1)} all-gather(bf16[1,4,6]{2,1,0:T(4,128)(2,1)S(1)} %bitcast.31), channel_id=1, replica_groups=mesh['grp'=16,'shard'=32] {'shard'}, dimensions={0}, use_global_device_ids=true | all-gather | bytes 1584 | tf_op jit(solution)/shard_map/all_gather | solution.py:22
  117.5 0.1 copy.19
  118.2 0.0 copy-done.1
  118.3 0.6 gather_fusion.1
  118.9 0.1 select_convert_fusion
  118.9 61.3 %all-gather.7.cloned.1.call-done = bf16[6,128,5376]{2,0,1:T(8,128)(2,1)} async-done(((bf16[6,4,5376]{2,0,1:T(8,128)(2,1)}), bf16[6,128,5376]{2,0,1:T(8,128)(2,1)}) %all-gather.7.cloned.1.call-update) | async-done | bytes 8257552 | tf_op jit(solution)/shard_map/all_gather | solution.py:21
  180.2 8.4 %fusion = f32[6,128,3,128]{3,1,2,0:T(8,128)S(1)} fusion(bf16[6,128,5376,1]{2,0,1,3:T(8,128)(2,1)} %bitcast.35, bf16[1,1,3,5376,128]{4,3,2,1,0:T(8,128)(2,1)} %param.8), kind=kOutput, calls=%fused_computation.4 | convolution fusion | flops 3170893824 | bytes 13565952 | tf_op jit(solution)/shard_map/rd,edc->rec/dot_general | solution.py:36
  188.6 0.7 gather_fusion.3
  189.3 1.2 fusion.4
  (5 shorter events, 0.0 us)
Async XLA Ops:
  6.5 60.4 %copy-start = (bf16[8,4]{0,1:T(4,128)(2,1)S(1)}, bf16[8,4]{0,1:T(4,128)(2,1)}, u32[]{:S(2)}) copy-start(bf16[8,4]{0,1:T(4,128)(2,1)} %param.7) | copy-start | bytes 196
  6.5 56.1 %all-gather.5.cloned.1.call-start = ((), (), s32[]{:S(2)}) async-start(), calls=%async_computation | async-start | bytes 5849088 | tf_op jit(solution)/shard_map/all_gather | solution.py:13
  7.3 111.0 %copy-start.1 = (s32[1,1,18,2]{2,3,1,0:T(2,128)S(1)}, s32[1,1,18,2]{2,3,1,0:T(2,128)}, u32[]{:S(2)}) copy-start(s32[1,1,18,2]{2,3,1,0:T(2,128)} %param.10) | copy-start | bytes 436
  7.3 172.9 %all-gather.7.cloned.1.call-start = ((), (), s32[]{:S(2)}) async-start(), calls=%async_computation.1 | async-start | bytes 11354112 | tf_op jit(solution)/shard_map/all_gather | solution.py:21
Sparse Core Ops, SparseCore 0:
  9.5 53.1 all-gather.4
  67.1 113.0 all-gather.6
where the time goes:
time: 198 us; the launch traced here: 197 us
  waiting for transfers between devices  115 us (58%)
  blocking collectives  49.6 us (25%)
  between operations  14.2 us (7%)
  matrix products  8.42 us (4%)
  local copies, waits for them, and re-layouts  6.26 us (3%)
  other arithmetic  3.4 us (2%)
    all_gather x1, waiting for transfers between devices, local(): lax.all_gather(slot_rows, 'shard', axis=1, tiled=True)  61.3 us
    all_gather x1, waiting for transfers between devices, local(): lax.all_gather(src_rows, 'grp', axis=0, tiled=True)  53.5 us
    all_gather x1, blocking collectives, local(): lax.all_gather(slot_scale, 'shard', axis=1, tiled=True)  33.3 us
    all_gather x1, blocking collectives, local(): lax.all_gather(src_act, 'grp', axis=0, tiled=True)  16.3 us
    dot_general x1, matrix products, local(): jnp.einsum('rd,edc->rec', stacked, weights, preferred_element_type=jnp.fl...  8.42 us
  transfers between devices with their start and end apart: 2, of which 2 were waited for; matrix products, arithmetic and copies ran while one was open for 2% of the time, Pallas kernels for 0%

commit v1 on v0

--- a/solution.py
+++ b/solution.py
@@ -2,6 +2,13 @@
 import jax.numpy as jnp
 from jax import lax
 from jax.sharding import PartitionSpec as P
+
+
+def all_by_exchange(x, axis, dim):
+    n_dev = lax.axis_size(axis)
+    parts = jnp.stack([x for _ in range(n_dev)])
+    parts = lax.all_to_all(parts, axis, split_axis=0, concat_axis=0)
+    return jnp.concatenate(parts, axis=dim)
 
 
 def local(src_rows, src_act, encoder, dest_list, pair_list, pair_count):
@@ -18,7 +25,7 @@
     slot_rows = jnp.where(is_valid[:, None, None], slot_rows, jnp.zeros((), slot_rows.dtype))
     slot_scale = jnp.where(is_valid[:, None], slot_scale, jnp.zeros((), slot_scale.dtype))
     full_rows, full_scale = (
-        lax.all_gather(slot_rows, "shard", axis=1, tiled=True),
+        all_by_exchange(slot_rows, "shard", 1),
         lax.all_gather(slot_scale, "shard", axis=1, tiled=True),
     )
     weights = encoder[0, 0]

time: 198 us -> 347 us (1.75); the launches traced: 197 us -> 342 us
  blocking collectives: 49.6 us -> 220 us
  waiting for transfers between devices: 115 us -> 54.3 us
  local copies, waits for them, and re-layouts: 6.26 us -> 31.7 us
  starting transfers between devices: 0.04 us -> 9.5 us
    all_gather x1, blocking collectives: 33.3 us -> 204 us  [local(): lax.all_gather(slot_scale, 'shard', axis=1, tiled=True)]
    all_gather x1 -> x0, waiting for transfers between devices: 61.3 us -> none  [local(): lax.all_gather(slot_rows, 'shard', axis=1, tiled=True)]
    dot_general x0 -> x1, local copies, waits for them, and re-layouts: none -> 12.9 us  [local(): jnp.einsum('rd,edc->rec', stacked, weights, preferred_element_type=jnp.fl...]
    all_to_all x0 -> x1, starting transfers between devices: none -> 9.5 us  [all_by_exchange(): parts = lax.all_to_all(parts, axis, split_axis=0, concat_axis=0)]
    reshape x0 -> x1, local copies, waits for them, and re-layouts: none -> 8.05 us  [all_by_exchange(): return jnp.concatenate(parts, axis=dim)]
    another operation x0 -> x1, local copies, waits for them, and re-layouts: none -> 5.31 us  [all_by_exchange(): parts = jnp.stack([x for _ in range(n_dev)])]
  transfers between devices with their start and end apart: 2 -> 2, of which waited for: 2 -> 1; matrix products, arithmetic and copies ran while one was open for 2% -> 1% of each run, Pallas kernels for 0% -> 0%
where the time goes in v1:
time: 347 us; the launch traced here: 342 us
  blocking collectives  220 us (63%)
  waiting for transfers between devices  54.3 us (16%)
  local copies, waits for them, and re-layouts  31.7 us (9%)
  between operations  14.2 us (4%)
  starting transfers between devices  9.5 us (3%)
  matrix products  8.04 us (2%)
    all_gather x1, blocking collectives, local(): lax.all_gather(slot_scale, 'shard', axis=1, tiled=True)  204 us
    all_gather x1, waiting for transfers between devices, local(): lax.all_gather(src_rows, 'grp', axis=0, tiled=True)  53.6 us
    all_gather x1, blocking collectives, local(): lax.all_gather(src_act, 'grp', axis=0, tiled=True)  16.6 us
    dot_general x1, local copies, waits for them, and re-layouts, local(): jnp.einsum('rd,edc->rec', stacked, weights, preferred_element_type=jnp.fl...  12.9 us
    all_to_all x1, starting transfers between devices, all_by_exchange(): parts = lax.all_to_all(parts, axis, split_axis=0, concat_axis=0)  9.5 us
    reshape x1, local copies, waits for them, and re-layouts, all_by_exchange(): return jnp.concatenate(parts, axis=dim)  8.05 us
    dot_general x1, matrix products, local(): jnp.einsum('rd,edc->rec', stacked, weights, preferred_element_type=jnp.fl...  8.04 us
  transfers between devices with their start and end apart: 2, of which 1 were waited for; matrix products, arithmetic and copies ran while one was open for 1% of the time, Pallas kernels for 0%

profile of v1, /device:TPU:1, one launch (start us, length us, event | category | flops | bytes accessed | tf_op | source)
XLA Modules:
  0.0 341.6 jit_solution(13191892886071272160)
XLA Ops:
  6.5 0.0 all-gather.4.cloned.1.call-start
  6.5 0.7 all-gather.4.cloned.1.call-update
  7.3 0.9 maximum_reduce_fusion
  8.1 0.9 compare_reduce_fusion.1
  9.1 53.6 %all-gather.4.cloned.1.call-done = bf16[128,4,5376]{2,1,0:T(4,128)(2,1)} async-done(((bf16[8,4,5376]{2,1,0:T(4,128)(2,1)}), bf16[128,4,5376]{2,1,0:T(4,128)(2,1)}) %all-gather.4.cloned.1.call-update) | async-done | bytes 5505040 | tf_op jit(solution)/shard_map/all_gather | solution.py:20
  62.6 3.3 gather_fusion.2
  65.9 0.2 select_select_fusion
  66.2 5.3 %stack.2 = bf16[32,6,4,5376]{3,2,1,0:T(4,128)(2,1)} broadcast(bf16[6,4,5376]{2,1,0:T(4,128)(2,1)S(1)} %select_select_fusion), dimensions={1,2,3} | broadcast | bytes 8515584 | tf_op jit(solution)/shard_map/stack | solution.py:9
  71.5 0.0 copy-start
  71.5 0.0 copy-start.1
  71.5 9.5 %all-to-all-start = ((bf16[32,6,4,5376]{3,2,1,0:T(4,128)(2,1)}), bf16[32,6,4,5376]{3,2,1,0:T(4,128)(2,1)}, u32[]{:S(2)}, u32[]{:S(2)}) async-start(bf16[32,6,4,5376]{3,2,1,0:T(4,128)(2,1)} %stack.2), calls=%async_computation | async-start | bytes 16515072 | tf_op jit(solution)/shard_map/all_to_all | solution.py:10
  81.0 0.0 copy-done
  81.0 16.6 %all-gather = bf16[16,8,4]{1,2,0:T(4,128)(2,1)S(1)} all-gather(bf16[1,8,4]{1,2,0:T(4,128)(2,1)S(1)} %bitcast.35), channel_id=1, replica_groups=mesh['grp'=16,'shard'=32] {'grp'}, dimensions={0}, use_global_device_ids=true | all-gather | bytes 1088 | tf_op jit(solution)/shard_map/all_gather | solution.py:21
  97.6 0.2 copy.13
  97.8 0.6 gather_fusion
  98.3 0.1 select_bitcast_fusion
  98.4 0.1 copy.14
  98.5 203.9 %all-gather.1 = bf16[32,4,6]{2,1,0:T(4,128)(2,1)S(1)} all-gather(bf16[1,4,6]{2,1,0:T(4,128)(2,1)S(1)} %bitcast.34), channel_id=1, replica_groups=mesh['grp'=16,'shard'=32] {'shard'}, dimensions={0}, use_global_device_ids=true | all-gather | bytes 1584 | tf_op jit(solution)/shard_map/all_gather | solution.py:29
  302.4 0.1 copy.18
  303.2 0.0 copy-done.1
  303.2 0.6 gather_fusion.1
  303.8 0.1 select_convert_fusion
  303.9 0.0 all-to-all-done
  303.9 8.1 %copy.16 = bf16[6,32,4,5376]{3,2,1,0:T(4,128)(2,1)} copy(bf16[6,32,4,5376]{3,2,0,1:T(4,128)(2,1)} %bitcast.10) | data formatting | bytes 16515072 | tf_op jit(solution)/shard_map/reshape | solution.py:11
  311.9 12.9 %reshape.120 = bf16[6,128,5376,1]{2,1,0,3:T(8,128)(2,1)} reshape(bf16[6,32,4,5376]{3,2,1,0:T(4,128)(2,1)} %copy.16) | data formatting | bytes 16515072 | tf_op jit(solution)/shard_map/rd,edc->rec/dot_general | solution.py:43
  324.8 8.0 %fusion = f32[6,128,3,128]{3,1,2,0:T(8,128)S(1)} fusion(bf16[6,128,5376,1]{2,1,0,3:T(8,128)(2,1)} %reshape.120, bf16[1,1,3,5376,128]{4,3,2,1,0:T(8,128)(2,1)} %param.8), kind=kOutput, calls=%fused_computation.4 | convolution fusion | flops 3170893824 | bytes 13565952 | tf_op jit(solution)/shard_map/rd,edc->rec/dot_general | solution.py:43
  332.9 0.7 gather_fusion.3
  333.5 1.2 fusion.4
  (5 shorter events, 0.0 us)
Async XLA Ops:
  6.5 56.1 %all-gather.4.cloned.1.call-start = ((), (), s32[]{:S(2)}) async-start(), calls=%async_computation.1 | async-start | bytes 5849088 | tf_op jit(solution)/shard_map/all_gather | solution.py:20
  71.5 9.5 %copy-start = (bf16[8,4]{0,1:T(4,128)(2,1)S(1)}, bf16[8,4]{0,1:T(4,128)(2,1)}, u32[]{:S(2)}) copy-start(bf16[8,4]{0,1:T(4,128)(2,1)} %param.7) | copy-start | bytes 196
  71.5 231.7 %copy-start.1 = (s32[1,1,18,2]{2,3,1,0:T(2,128)S(1)}, s32[1,1,18,2]{2,3,1,0:T(2,128)}, u32[]{:S(2)}) copy-start(s32[1,1,18,2]{2,3,1,0:T(2,128)} %param.10) | copy-start | bytes 436
  71.5 232.4 %all-to-all-start = ((bf16[32,6,4,5376]{3,2,1,0:T(4,128)(2,1)}), bf16[32,6,4,5376]{3,2,1,0:T(4,128)(2,1)}, u32[]{:S(2)}, u32[]{:S(2)}) async-start(bf16[32,6,4,5376]{3,2,1,0:T(4,128)(2,1)} %stack.2), calls=%async_computation | async-start | bytes 16515072 | tf_op jit(solution)/shard_map/all_to_all | solution.py:10
Sparse Core Ops, SparseCore 0:
  9.5 53.1 all-gather.3
